TPU v7x, 32 devices: a whole 2x2x4 slice. The times are simulated.
32 devices in a mesh: groups: 2 (over y), row: 16 (over z, x, core).
Axes of the slice: x: 2, y: 2, z: 4, core: 2. Of those that a mesh axis runs over, the one named last changes fastest.
Arguments:
- features: bfloat16 [576, 16384], P(None, ('groups', 'row')), parts along dimension 1, may hold values from -150 to 150
- labels: int32 [16384], P(('groups', 'row')), parts along dimension 0, may hold values 0 or 1
- other_predictor: float32 [16384], P(('groups', 'row')), parts along dimension 0, may hold values from -6 to 6
- coefficients: float32 [8192], P('groups'), parts along dimension 0, may hold values from -0.09375 to 0.09375
- panel_block: int32 [2], P('groups'), parts along dimension 0, may hold values from 0 to 55
Outputs:
- r_factor: float32 [1152, 576], P('groups'), parts along dimension 0
- residual: float32 [16384], P(('groups', 'row')), parts along dimension 0
There are 2 independent parts, one for each index of `groups`. A program takes and returns all parts, laid end to end along the dimension named above; each array names one. Nothing has to cross between parts.
All inputs are finite; a program needn't handle non-finite values. No bound on the sum of `labels` on one device may be relied on, other than what follows from the above.
Results may differ from a plain program's by a relative error of at most 0.0003.
Values sent between devices are 32-bit elements; how exact they have to be, the bound alone decides.
No kernel may reach another device: no remote copies, remote signals or barrier semaphores. Data moves between devices by JAX's collectives and lax.ppermute only.
A program may use at most 64 MiB of HBM per device.

v0:
```python
import math
import jax
import jax.numpy as jnp
from jax import lax
from jax.sharding import PartitionSpec as P

PB = 64
precise = lax.Precision.HIGHEST


def joined(array, axis, combine):
    everything = lax.all_gather(array, axis)
    leading = everything[0]

    def lap(k, so_far):
        return combine(so_far, everything[k])

    return lax.fori_loop(1, lax.axis_size(axis), lap, leading)


def inner_rows(left_rows, right_rows):
    return lax.dot_general(left_rows, right_rows, (((1,), (1,)), ((), ())), precision=precise)


def upper_merge(earlier, another):
    gram_total = jnp.dot(earlier.T, earlier, precision=precise) + jnp.dot(
        another.T, another, precision=precise
    )
    return jnp.linalg.cholesky(gram_total).T


def panel_lower(panel_rows):
    local_gram = inner_rows(panel_rows, panel_rows)
    upper_factor = joined(jnp.linalg.cholesky(local_gram).T, "row", upper_merge)
    return upper_factor.T


def shards(features, labels, other_predictor, coefficients, panel_block):
    window, rows_here = features.shape
    total_rows = rows_here * lax.axis_size("row")
    first_col = panel_block[0] * PB
    window_coef = lax.dynamic_slice(coefficients, (first_col,), (window,))
    as_float = features.astype(jnp.float32)
    linear = jnp.dot(window_coef, as_float, precision=precise) + other_predictor
    fitted = jax.nn.sigmoid(linear)
    weight = jnp.maximum(fitted * (1.0 - fitted), 0.01)
    root_weight = jnp.sqrt(weight)
    norm_scale = 1.0 / math.sqrt(total_rows)
    scaled = as_float * (root_weight * norm_scale)[None, :]
    target = (
        root_weight * linear + (labels.astype(jnp.float32) - fitted) / root_weight
    ) * norm_scale
    working = jnp.concatenate([scaled, target[None, :]], axis=0)
    panels = window // PB
    blocks = []
    for step in range(panels):
        panel_rows = working[:PB]
        trailing = working[PB:]
        lower_factor = panel_lower(panel_rows)
        orthonormal = lax.linalg.triangular_solve(
            lower_factor, panel_rows, left_side=True, lower=True
        )
        coupling = lax.psum(inner_rows(orthonormal, trailing), "row")
        working = trailing - jnp.dot(coupling.T, orthonormal, precision=precise)
        blocks.append(
            jnp.concatenate(
                [jnp.zeros((PB, step * PB), jnp.float32), lower_factor.T, coupling[:, :-1]], axis=1
            )
        )
    return (jnp.concatenate(blocks, axis=0), working[0] * math.sqrt(total_rows))


def solution(mesh):
    in_specs = (
        P(None, ("groups", "row")),
        P(("groups", "row")),
        P(("groups", "row")),
        P("groups"),
        P("groups"),
    )
    out_specs = (P("groups", None), P(("groups", "row")))
    return jax.shard_map(shards, mesh=mesh, in_specs=in_specs, out_specs=out_specs, check_vma=False)
```

profile of v0, /device:TPU:0, one launch (start us, length us, event | category | flops | bytes accessed | tf_op | source)
XLA Modules:
  0.0 2036.4 jit_solution(737754866576527121)
XLA Ops:
  12.4 5.8 cholesky.383
  19.6 24.6 %all-gather = f32[1024,64]{1,0:T(8,128)S(1)} all-gather(f32[64,64]{1,0:T(8,128)S(1)} %copy.89), channel_id=2, replica_groups=mesh['groups'=2,'row'=16] {'row'}, dimensions={0}, use_global_device_ids=true | all-gather | bytes 278528 | tf_op jit(solution)/shard_map/all_gather | solution.py:12
  44.3 116.1 %while.135 = (s32[]{:T(128)}, f32[64,64]{0,1:T(8,128)S(1)}, f32[16,64,64]{2,1,0:T(8,128)S(1)}, s32[]{:T(128)}, s32[]{:T(128)}, /*index=5*/s32[]{:T(128)}) while((s32[]{:T(128)}, f32[64,64]{0,1:T(8,128)S(1)}, f32[16,64,64]{2,1,0:T(8,128)S(1)}, s32[]{:T(128)}, s32[]{:T(128)}, /*index=5*/s32[]{:T(128)}) %tuple.347), condition=%wide.region_3.0_spmd, body=%wide.region_2.0_spmd.sunk | while | flops 6328388 | bytes 246389 | solution.py:18
  44.9 5.8 cholesky.862
  60.3 5.8 cholesky.862
  99.1 5.8 cholesky.862
  114.6 5.8 cholesky.862
  167.9 86.1 %all-reduce.7.cloned.1.call-done = f32[64,513]{1,0:T(8,128)} async-done(((f32[64,513]{1,0:T(8,128)}), f32[64,513]{1,0:T(8,128)}) %all-reduce.7.cloned.1.call-update) | async-done | bytes 131344 | tf_op jit(solution)/shard_map/psum | solution.py:63
  263.5 22.8 %all-gather.1 = f32[1024,64]{1,0:T(8,128)S(1)} all-gather(f32[64,64]{1,0:T(8,128)S(1)} %copy.93), channel_id=3, replica_groups=mesh['groups'=2,'row'=16] {'row'}, dimensions={0}, use_global_device_ids=true | all-gather | bytes 278528 | tf_op jit(solution)/shard_map/all_gather | solution.py:12
  286.4 116.1 %while.136 = (s32[]{:T(128)}, f32[64,64]{0,1:T(8,128)S(1)}, f32[16,64,64]{2,1,0:T(8,128)S(1)}, s32[]{:T(128)}, s32[]{:T(128)}, /*index=5*/s32[]{:T(128)}) while((s32[]{:T(128)}, f32[64,64]{0,1:T(8,128)S(1)}, f32[16,64,64]{2,1,0:T(8,128)S(1)}, s32[]{:T(128)}, s32[]{:T(128)}, /*index=5*/s32[]{:T(128)}) %tuple.348), condition=%wide.region_6.9_spmd, body=%wide.region_5.8_spmd.sunk | while | flops 6328388 | bytes 246389 | solution.py:18
  410.8 84.3 %all-reduce.9.cloned.1.call-done = f32[64,449]{1,0:T(8,128)} async-done(((f32[64,449]{1,0:T(8,128)}), f32[64,449]{1,0:T(8,128)}) %all-reduce.9.cloned.1.call-update) | async-done | bytes 114960 | tf_op jit(solution)/shard_map/psum | solution.py:63
  504.5 23.4 %all-gather.2 = f32[1024,64]{1,0:T(8,128)S(1)} all-gather(f32[64,64]{1,0:T(8,128)S(1)} %copy.97), channel_id=4, replica_groups=mesh['groups'=2,'row'=16] {'row'}, dimensions={0}, use_global_device_ids=true | all-gather | bytes 278528 | tf_op jit(solution)/shard_map/all_gather | solution.py:12
  528.0 116.1 %while.137 = (s32[]{:T(128)}, f32[64,64]{0,1:T(8,128)S(1)}, f32[16,64,64]{2,1,0:T(8,128)S(1)}, s32[]{:T(128)}, s32[]{:T(128)}, /*index=5*/s32[]{:T(128)}) while((s32[]{:T(128)}, f32[64,64]{0,1:T(8,128)S(1)}, f32[16,64,64]{2,1,0:T(8,128)S(1)}, s32[]{:T(128)}, s32[]{:T(128)}, /*index=5*/s32[]{:T(128)}) %tuple.349), condition=%wide.region_9.12_spmd, body=%wide.region_8.11_spmd.sunk | while | flops 6328388 | bytes 246389 | solution.py:18
  651.8 84.8 %all-reduce.11.cloned.1.call-done = f32[64,385]{1,0:T(8,128)} async-done(((f32[64,385]{1,0:T(8,128)}), f32[64,385]{1,0:T(8,128)}) %all-reduce.11.cloned.1.call-update) | async-done | bytes 98576 | tf_op jit(solution)/shard_map/psum | solution.py:63
  746.0 23.4 %all-gather.3 = f32[1024,64]{1,0:T(8,128)S(1)} all-gather(f32[64,64]{1,0:T(8,128)S(1)} %copy.101), channel_id=5, replica_groups=mesh['groups'=2,'row'=16] {'row'}, dimensions={0}, use_global_device_ids=true | all-gather | bytes 278528 | tf_op jit(solution)/shard_map/all_gather | solution.py:12
  769.5 116.1 %while.138 = (s32[]{:T(128)}, f32[64,64]{0,1:T(8,128)S(1)}, f32[16,64,64]{2,1,0:T(8,128)S(1)}, s32[]{:T(128)}, s32[]{:T(128)}, /*index=5*/s32[]{:T(128)}) while((s32[]{:T(128)}, f32[64,64]{0,1:T(8,128)S(1)}, f32[16,64,64]{2,1,0:T(8,128)S(1)}, s32[]{:T(128)}, s32[]{:T(128)}, /*index=5*/s32[]{:T(128)}) %tuple.350), condition=%wide.region_12.15_spmd, body=%wide.region_11.14_spmd.sunk | while | flops 6328388 | bytes 246389 | solution.py:18
  893.3 85.0 %all-reduce.13.cloned.1.call-done = f32[64,321]{1,0:T(8,128)} async-done(((f32[64,321]{1,0:T(8,128)}), f32[64,321]{1,0:T(8,128)}) %all-reduce.13.cloned.1.call-update) | async-done | bytes 82192 | tf_op jit(solution)/shard_map/psum | solution.py:63
  987.6 20.8 %all-gather.4 = f32[1024,64]{1,0:T(8,128)S(1)} all-gather(f32[64,64]{1,0:T(8,128)S(1)} %copy.105), channel_id=6, replica_groups=mesh['groups'=2,'row'=16] {'row'}, dimensions={0}, use_global_device_ids=true | all-gather | bytes 278528 | tf_op jit(solution)/shard_map/all_gather | solution.py:12
  1008.5 116.1 %while.139 = (s32[]{:T(128)}, f32[64,64]{0,1:T(8,128)S(1)}, f32[16,64,64]{2,1,0:T(8,128)S(1)}, s32[]{:T(128)}, s32[]{:T(128)}, /*index=5*/s32[]{:T(128)}) while((s32[]{:T(128)}, f32[64,64]{0,1:T(8,128)S(1)}, f32[16,64,64]{2,1,0:T(8,128)S(1)}, s32[]{:T(128)}, s32[]{:T(128)}, /*index=5*/s32[]{:T(128)}) %tuple.351), condition=%wide.region_15.18_spmd, body=%wide.region_14.17_spmd.sunk | while | flops 6328388 | bytes 246389 | solution.py:18
  1132.1 85.3 %all-reduce.15.cloned.1.call-done = f32[64,257]{1,0:T(8,128)} async-done(((f32[64,257]{1,0:T(8,128)}), f32[64,257]{1,0:T(8,128)}) %all-reduce.15.cloned.1.call-update) | async-done | bytes 65808 | tf_op jit(solution)/shard_map/psum | solution.py:63
  1226.6 20.8 %all-gather.5 = f32[1024,64]{1,0:T(8,128)S(1)} all-gather(f32[64,64]{1,0:T(8,128)S(1)} %copy.109), channel_id=7, replica_groups=mesh['groups'=2,'row'=16] {'row'}, dimensions={0}, use_global_device_ids=true | all-gather | bytes 278528 | tf_op jit(solution)/shard_map/all_gather | solution.py:12
  1247.5 116.1 %while.140 = (s32[]{:T(128)}, f32[64,64]{0,1:T(8,128)S(1)}, f32[16,64,64]{2,1,0:T(8,128)S(1)}, s32[]{:T(128)}, s32[]{:T(128)}, /*index=5*/s32[]{:T(128)}) while((s32[]{:T(128)}, f32[64,64]{0,1:T(8,128)S(1)}, f32[16,64,64]{2,1,0:T(8,128)S(1)}, s32[]{:T(128)}, s32[]{:T(128)}, /*index=5*/s32[]{:T(128)}) %tuple.352), condition=%wide.region_18.21_spmd, body=%wide.region_17.20_spmd.sunk | while | flops 6328388 | bytes 246389 | solution.py:18
  1369.4 57.9 %psum.68 = f32[64,193]{1,0:T(8,128)S(1)} all-reduce(f32[64,193]{1,0:T(8,128)S(1)} %fusion.46), channel_id=1, replica_groups=mesh['groups'=2,'row'=16] {'row'}, use_global_device_ids=true, to_apply=%region_19.22 | all-reduce | flops 12352 | bytes 98816 | tf_op jit(solution)/shard_map/psum | solution.py:63
  1435.5 18.9 all-gather.6
  1454.5 116.1 %while.141 = (s32[]{:T(128)}, f32[64,64]{0,1:T(8,128)S(1)}, f32[16,64,64]{2,1,0:T(8,128)S(1)}, s32[]{:T(128)}, s32[]{:T(128)}, /*index=5*/s32[]{:T(128)}) while((s32[]{:T(128)}, f32[64,64]{0,1:T(8,128)S(1)}, f32[16,64,64]{2,1,0:T(8,128)S(1)}, s32[]{:T(128)}, s32[]{:T(128)}, /*index=5*/s32[]{:T(128)}) %tuple.353), condition=%wide.region_21.24_spmd, body=%wide.region_20.23_spmd.sunk | while | flops 6328388 | bytes 246389 | solution.py:18
  1576.3 59.9 %psum.69 = f32[64,129]{1,0:T(8,128)S(1)} all-reduce(f32[64,129]{1,0:T(8,128)S(1)} %fusion.48), channel_id=1, replica_groups=mesh['groups'=2,'row'=16] {'row'}, use_global_device_ids=true, to_apply=%region_22.25 | all-reduce | flops 8256 | bytes 66048 | tf_op jit(solution)/shard_map/psum | solution.py:63
  1644.3 18.7 all-gather.7
  1663.1 116.1 %while.142 = (s32[]{:T(128)}, f32[64,64]{0,1:T(8,128)S(1)}, f32[16,64,64]{2,1,0:T(8,128)S(1)}, s32[]{:T(128)}, s32[]{:T(128)}, /*index=5*/s32[]{:T(128)}) while((s32[]{:T(128)}, f32[64,64]{0,1:T(8,128)S(1)}, f32[16,64,64]{2,1,0:T(8,128)S(1)}, s32[]{:T(128)}, s32[]{:T(128)}, /*index=5*/s32[]{:T(128)}) %tuple.354), condition=%wide.region_24.27_spmd, body=%wide.region_23.26_spmd.sunk | while | flops 6328388 | bytes 246389 | solution.py:18
  1784.7 59.9 %psum.70 = f32[64,65]{1,0:T(8,128)S(1)} all-reduce(f32[64,65]{1,0:T(8,128)S(1)} %fusion.50), channel_id=1, replica_groups=mesh['groups'=2,'row'=16] {'row'}, use_global_device_ids=true, to_apply=%region_25.28 | all-reduce | flops 4160 | bytes 33280 | tf_op jit(solution)/shard_map/psum | solution.py:63
  1852.6 18.7 all-gather.8
  1871.3 116.1 %while.143 = (s32[]{:T(128)}, f32[64,64]{0,1:T(8,128)S(1)}, f32[16,64,64]{2,1,0:T(8,128)S(1)}, s32[]{:T(128)}, s32[]{:T(128)}, /*index=5*/s32[]{:T(128)}) while((s32[]{:T(128)}, f32[64,64]{0,1:T(8,128)S(1)}, f32[16,64,64]{2,1,0:T(8,128)S(1)}, s32[]{:T(128)}, s32[]{:T(128)}, /*index=5*/s32[]{:T(128)}) %tuple.346), condition=%wide.region_27.30_spmd, body=%wide.region_26.29_spmd.sunk | while | flops 6328388 | bytes 246389 | solution.py:18
  1993.3 31.9 %psum.71 = f32[64]{0:T(128)S(1)} all-reduce(f32[64]{0:T(128)S(1)} %convolution_bitcast_fusion), channel_id=1, replica_groups=mesh['groups'=2,'row'=16] {'row'}, use_global_device_ids=true, to_apply=%region_28.31 | all-reduce | flops 64 | bytes 512 | tf_op jit(solution)/shard_map/psum | solution.py:63
  (1270 shorter events, 1156.7 us)
Async XLA Ops:
  7.2 246.8 %all-reduce.7.cloned.1.call-start = ((), (), s32[]{:S(2)}) async-start(), calls=%async_computation | async-start | bytes 327680 | tf_op jit(solution)/shard_map/psum | solution.py:63
  167.6 327.4 %all-reduce.9.cloned.1.call-start = ((), (), s32[]{:S(2)}) async-start(), calls=%async_computation.1 | async-start | bytes 262144 | tf_op jit(solution)/shard_map/psum | solution.py:63
  402.5 7.4 slice-start
  409.4 327.2 %all-reduce.11.cloned.1.call-start = ((), (), s32[]{:S(2)}) async-start(), calls=%async_computation.2 | async-start | bytes 262144 | tf_op jit(solution)/shard_map/psum | solution.py:63
  644.1 6.8 copy-start
  650.9 327.4 %all-reduce.13.cloned.1.call-start = ((), (), s32[]{:S(2)}) async-start(), calls=%async_computation.3 | async-start | bytes 196608 | tf_op jit(solution)/shard_map/psum | solution.py:63
  885.6 6.8 slice-start.2
  892.2 325.2 %all-reduce.15.cloned.1.call-start = ((), (), s32[]{:S(2)}) async-start(), calls=%async_computation.4 | async-start | bytes 196608 | tf_op jit(solution)/shard_map/psum | solution.py:63
  1124.6 6.6 copy-start.2
  1636.2 351.5 %copy-start.1 = (f32[64,129]{1,0:T(8,128)}, f32[64,129]{1,0:T(8,128)S(1)}, u32[]{:S(2)}) copy-start(f32[64,129]{1,0:T(8,128)S(1)} %psum.69) | copy-start | bytes 99076
  1871.3 154.6 %slice-start.3 = ((f32[64,257]{1,0:T(8,128)}), f32[64,256]{1,0:T(8,128)S(1)}, s32[]{:S(2)}) async-start(f32[64,257]{1,0:T(8,128)} %all-reduce.15.cloned.1.call-done), calls=%async_computation.8 | async-start | bytes 131072 | tf_op jit(solution)/shard_map/slice | solution.py:67
  1987.7 39.7 %slice-start.1 = ((f32[64,129]{1,0:T(8,128)}), f32[64,128]{1,0:T(8,128)S(1)}, s32[]{:S(2)}) async-start(f32[64,129]{1,0:T(8,128)} %copy-done.1), calls=%async_computation.6 | async-start | bytes 65536 | tf_op jit(solution)/shard_map/slice | solution.py:67
Sparse Core Ops, SparseCore 0:
  167.7 86.1 all-reduce.6
  409.5 85.4 all-reduce.8
  651.0 85.5 all-reduce.10
  892.4 85.9 all-reduce.12
  1131.4 85.9 all-reduce.14
where the time goes:
time: 2050 us; the launch traced here: 2040 us
  other arithmetic  1090 us (53%)
  waiting for transfers between devices  426 us (21%)
  blocking collectives  402 us (20%)
  matrix products  84.3 us (4%)
    another operation x405, other arithmetic, upper_merge(): return jnp.linalg.cholesky(gram_total).T  880 us
    psum x5, waiting for transfers between devices, shards(): coupling = lax.psum(inner_rows(orthonormal, trailing), 'row')  425 us
    psum x4, blocking collectives, shards(): coupling = lax.psum(inner_rows(orthonormal, trailing), 'row')  210 us
    all_gather x9, blocking collectives, joined(): everything = lax.all_gather(array, axis)  192 us
    transpose x135, other arithmetic, upper_merge(): return jnp.linalg.cholesky(gram_total).T  88 us
    another operation x27, other arithmetic, panel_lower(): upper_factor = joined(jnp.linalg.cholesky(local_gram).T, 'row', upper_merge)  58.7 us
    another operation x18, other arithmetic, shards(): lax.linalg.triangular_solve(lower_factor, panel_rows, left_side=True, low...  44.2 us
  transfers between devices with their start and end apart: 5, of which 5 were waited for; matrix products, arithmetic and copies ran while one was open for 0% of the time, Pallas kernels for 0%

commit v1 on v0

--- a/solution.py
+++ b/solution.py
@@ -6,6 +6,11 @@
 
 PB = 64
 precise = lax.Precision.HIGHEST
+
+
+def _plan_blocks(here_x, a_name):
+    arr_next = jnp.sum(jax.lax.all_gather(here_x, a_name), 0)
+    return arr_next
 
 
 def joined(array, axis, combine):
@@ -60,7 +65,7 @@
         orthonormal = lax.linalg.triangular_solve(
             lower_factor, panel_rows, left_side=True, lower=True
         )
-        coupling = lax.psum(inner_rows(orthonormal, trailing), "row")
+        coupling = _plan_blocks(inner_rows(orthonormal, trailing), "row")
         working = trailing - jnp.dot(coupling.T, orthonormal, precision=precise)
         blocks.append(
             jnp.concatenate(

time: 2050 us -> 1690 us (0.82)
  waiting for transfers between devices: 426 us -> 189 us
  blocking collectives: 402 us -> 282 us
    psum x5 -> x0, waiting for transfers between devices: 425 us -> none  [shards(): coupling = lax.psum(inner_rows(orthonormal, trailing), 'row')]
    psum x4 -> x0, blocking collectives: 210 us -> none  [shards(): coupling = lax.psum(inner_rows(orthonormal, trailing), 'row')]
    all_gather x0 -> x5, waiting for transfers between devices: none -> 189 us  [_plan_blocks(): arr_next = jnp.sum(jax.lax.all_gather(here_x, a_name), 0)]
    all_gather x0 -> x3, blocking collectives: none -> 60.7 us  [_plan_blocks(): arr_next = jnp.sum(jax.lax.all_gather(here_x, a_name), 0)]
    unnamed x0 -> x1, blocking collectives: none -> 29.8 us
where the time goes in v1:
time: 1690 us; the launch traced here: 1680 us
  other arithmetic  1090 us (64%)
  blocking collectives  282 us (17%)
  waiting for transfers between devices  189 us (11%)
  matrix products  79.9 us (5%)
    another operation x405, other arithmetic, upper_merge(): return jnp.linalg.cholesky(gram_total).T  880 us
    all_gather x9, blocking collectives, joined(): everything = lax.all_gather(array, axis)  191 us
    all_gather x5, waiting for transfers between devices, _plan_blocks(): arr_next = jnp.sum(jax.lax.all_gather(here_x, a_name), 0)  189 us
    transpose x135, other arithmetic, upper_merge(): return jnp.linalg.cholesky(gram_total).T  88 us
    all_gather x3, blocking collectives, _plan_blocks(): arr_next = jnp.sum(jax.lax.all_gather(here_x, a_name), 0)  60.7 us
    another operation x27, other arithmetic, panel_lower(): upper_factor = joined(jnp.linalg.cholesky(local_gram).T, 'row', upper_merge)  58.8 us
    another operation x18, other arithmetic, shards(): lax.linalg.triangular_solve(lower_factor, panel_rows, left_side=True, low...  44.1 us
  transfers between devices with their start and end apart: 5, of which 5 were waited for; matrix products, arithmetic and copies ran while one was open for 0% of the time, Pallas kernels for 0%

profile of v1, /device:TPU:0, one launch (start us, length us, event | category | flops | bytes accessed | tf_op | source)
XLA Modules:
  0.0 1683.4 jit_solution(14957985581196737208)
XLA Ops:
  12.4 5.8 cholesky.383
  19.6 24.6 %all-gather = f32[1024,64]{1,0:T(8,128)S(1)} all-gather(f32[64,64]{1,0:T(8,128)S(1)} %copy.152), channel_id=2, replica_groups=mesh['groups'=2,'row'=16] {'row'}, dimensions={0}, use_global_device_ids=true | all-gather | bytes 278528 | tf_op jit(solution)/shard_map/all_gather | solution.py:17
  44.3 116.1 %while.135 = (s32[]{:T(128)}, f32[64,64]{0,1:T(8,128)S(1)}, f32[16,64,64]{2,1,0:T(8,128)S(1)}, s32[]{:T(128)}, s32[]{:T(128)}, /*index=5*/s32[]{:T(128)}) while((s32[]{:T(128)}, f32[64,64]{0,1:T(8,128)S(1)}, f32[16,64,64]{2,1,0:T(8,128)S(1)}, s32[]{:T(128)}, s32[]{:T(128)}, /*index=5*/s32[]{:T(128)}) %tuple.356), condition=%wide.region_3.0_spmd, body=%wide.region_2.0_spmd.sunk | while | flops 6328388 | bytes 246389 | solution.py:23
  44.9 5.8 cholesky.862
  52.6 5.8 cholesky.862
  60.3 5.8 cholesky.862
  68.1 5.8 cholesky.862
  167.7 40.5 %all-gather.24.cloned.1.call-done = f32[1024,513]{1,0:T(8,128)} async-done(((f32[64,513]{1,0:T(8,128)}), f32[1024,513]{1,0:T(8,128)}) %all-gather.24.cloned.1.call-update) | async-done | bytes 2101264 | tf_op jit(solution)/shard_map/all_gather | solution.py:12
  218.7 20.7 %all-gather.2 = f32[1024,64]{1,0:T(8,128)S(1)} all-gather(f32[64,64]{1,0:T(8,128)S(1)} %copy.156), channel_id=4, replica_groups=mesh['groups'=2,'row'=16] {'row'}, dimensions={0}, use_global_device_ids=true | all-gather | bytes 278528 | tf_op jit(solution)/shard_map/all_gather | solution.py:17
  239.4 116.1 %while.136 = (s32[]{:T(128)}, f32[64,64]{0,1:T(8,128)S(1)}, f32[16,64,64]{2,1,0:T(8,128)S(1)}, s32[]{:T(128)}, s32[]{:T(128)}, /*index=5*/s32[]{:T(128)}) while((s32[]{:T(128)}, f32[64,64]{0,1:T(8,128)S(1)}, f32[16,64,64]{2,1,0:T(8,128)S(1)}, s32[]{:T(128)}, s32[]{:T(128)}, /*index=5*/s32[]{:T(128)}) %tuple.357), condition=%wide.region_6.9_spmd, body=%wide.region_5.8_spmd.sunk | while | flops 6328388 | bytes 246389 | solution.py:23
  362.7 38.6 %all-gather.26.cloned.1.call-done = f32[1024,449]{1,0:T(8,128)} async-done(((f32[64,449]{1,0:T(8,128)}), f32[1024,449]{1,0:T(8,128)}) %all-gather.26.cloned.1.call-update) | async-done | bytes 1839120 | tf_op jit(solution)/shard_map/all_gather | solution.py:12
  411.6 20.6 %all-gather.4 = f32[1024,64]{1,0:T(8,128)S(1)} all-gather(f32[64,64]{1,0:T(8,128)S(1)} %copy.160), channel_id=6, replica_groups=mesh['groups'=2,'row'=16] {'row'}, dimensions={0}, use_global_device_ids=true | all-gather | bytes 278528 | tf_op jit(solution)/shard_map/all_gather | solution.py:17
  432.3 116.1 %while.137 = (s32[]{:T(128)}, f32[64,64]{0,1:T(8,128)S(1)}, f32[16,64,64]{2,1,0:T(8,128)S(1)}, s32[]{:T(128)}, s32[]{:T(128)}, /*index=5*/s32[]{:T(128)}) while((s32[]{:T(128)}, f32[64,64]{0,1:T(8,128)S(1)}, f32[16,64,64]{2,1,0:T(8,128)S(1)}, s32[]{:T(128)}, s32[]{:T(128)}, /*index=5*/s32[]{:T(128)}) %tuple.358), condition=%wide.region_9.12_spmd, body=%wide.region_8.11_spmd.sunk | while | flops 6328388 | bytes 246389 | solution.py:23
  555.3 38.8 %all-gather.28.cloned.1.call-done = f32[1024,385]{1,0:T(8,128)} async-done(((f32[64,385]{1,0:T(8,128)}), f32[1024,385]{1,0:T(8,128)}) %all-gather.28.cloned.1.call-update) | async-done | bytes 1576976 | tf_op jit(solution)/shard_map/all_gather | solution.py:12
  604.3 20.6 %all-gather.6 = f32[1024,64]{1,0:T(8,128)S(1)} all-gather(f32[64,64]{1,0:T(8,128)S(1)} %copy.164), channel_id=8, replica_groups=mesh['groups'=2,'row'=16] {'row'}, dimensions={0}, use_global_device_ids=true | all-gather | bytes 278528 | tf_op jit(solution)/shard_map/all_gather | solution.py:17
  625.0 116.1 %while.138 = (s32[]{:T(128)}, f32[64,64]{0,1:T(8,128)S(1)}, f32[16,64,64]{2,1,0:T(8,128)S(1)}, s32[]{:T(128)}, s32[]{:T(128)}, /*index=5*/s32[]{:T(128)}) while((s32[]{:T(128)}, f32[64,64]{0,1:T(8,128)S(1)}, f32[16,64,64]{2,1,0:T(8,128)S(1)}, s32[]{:T(128)}, s32[]{:T(128)}, /*index=5*/s32[]{:T(128)}) %tuple.359), condition=%wide.region_12.15_spmd, body=%wide.region_11.14_spmd.sunk | while | flops 6328388 | bytes 246389 | solution.py:23
  748.0 36.7 %all-gather.30.cloned.1.call-done = f32[1024,321]{1,0:T(8,128)} async-done(((f32[64,321]{1,0:T(8,128)}), f32[1024,321]{1,0:T(8,128)}) %all-gather.30.cloned.1.call-update) | async-done | bytes 1314832 | tf_op jit(solution)/shard_map/all_gather | solution.py:12
  794.6 20.5 %all-gather.8 = f32[1024,64]{1,0:T(8,128)S(1)} all-gather(f32[64,64]{1,0:T(8,128)S(1)} %copy.168), channel_id=10, replica_groups=mesh['groups'=2,'row'=16] {'row'}, dimensions={0}, use_global_device_ids=true | all-gather | bytes 278528 | tf_op jit(solution)/shard_map/all_gather | solution.py:17
  815.2 116.1 %while.139 = (s32[]{:T(128)}, f32[64,64]{0,1:T(8,128)S(1)}, f32[16,64,64]{2,1,0:T(8,128)S(1)}, s32[]{:T(128)}, s32[]{:T(128)}, /*index=5*/s32[]{:T(128)}) while((s32[]{:T(128)}, f32[64,64]{0,1:T(8,128)S(1)}, f32[16,64,64]{2,1,0:T(8,128)S(1)}, s32[]{:T(128)}, s32[]{:T(128)}, /*index=5*/s32[]{:T(128)}) %tuple.360), condition=%wide.region_15.18_spmd, body=%wide.region_14.17_spmd.sunk | while | flops 6328388 | bytes 246389 | solution.py:23
  940.2 34.8 %all-gather.32.cloned.1.call-done = f32[1024,257]{1,0:T(8,128)} async-done(((f32[64,257]{1,0:T(8,128)}), f32[1024,257]{1,0:T(8,128)}) %all-gather.32.cloned.1.call-update) | async-done | bytes 1052688 | tf_op jit(solution)/shard_map/all_gather | solution.py:12
  984.9 20.6 %all-gather.10 = f32[1024,64]{1,0:T(8,128)S(1)} all-gather(f32[64,64]{1,0:T(8,128)S(1)} %copy.172), channel_id=12, replica_groups=mesh['groups'=2,'row'=16] {'row'}, dimensions={0}, use_global_device_ids=true | all-gather | bytes 278528 | tf_op jit(solution)/shard_map/all_gather | solution.py:17
  1005.5 116.1 %while.140 = (s32[]{:T(128)}, f32[64,64]{0,1:T(8,128)S(1)}, f32[16,64,64]{2,1,0:T(8,128)S(1)}, s32[]{:T(128)}, s32[]{:T(128)}, /*index=5*/s32[]{:T(128)}) while((s32[]{:T(128)}, f32[64,64]{0,1:T(8,128)S(1)}, f32[16,64,64]{2,1,0:T(8,128)S(1)}, s32[]{:T(128)}, s32[]{:T(128)}, /*index=5*/s32[]{:T(128)}) %tuple.361), condition=%wide.region_18.21_spmd, body=%wide.region_17.20_spmd.sunk | while | flops 6328388 | bytes 246389 | solution.py:23
  1127.5 21.1 %all-gather.11 = f32[1024,193]{1,0:T(8,128)S(1)} all-gather(f32[64,193]{1,0:T(8,128)S(1)} %fusion.46), channel_id=13, replica_groups=mesh['groups'=2,'row'=16] {'row'}, dimensions={0}, use_global_device_ids=true | all-gather | bytes 839936 | tf_op jit(solution)/shard_map/all_gather | solution.py:12
  1156.8 21.9 %all-gather.12 = f32[1024,64]{1,0:T(8,128)S(1)} all-gather(f32[64,64]{1,0:T(8,128)S(1)} %copy.176), channel_id=14, replica_groups=mesh['groups'=2,'row'=16] {'row'}, dimensions={0}, use_global_device_ids=true | all-gather | bytes 278528 | tf_op jit(solution)/shard_map/all_gather | solution.py:17
  1178.8 116.1 %while.141 = (s32[]{:T(128)}, f32[64,64]{0,1:T(8,128)S(1)}, f32[16,64,64]{2,1,0:T(8,128)S(1)}, s32[]{:T(128)}, s32[]{:T(128)}, /*index=5*/s32[]{:T(128)}) while((s32[]{:T(128)}, f32[64,64]{0,1:T(8,128)S(1)}, f32[16,64,64]{2,1,0:T(8,128)S(1)}, s32[]{:T(128)}, s32[]{:T(128)}, /*index=5*/s32[]{:T(128)}) %tuple.362), condition=%wide.region_21.24_spmd, body=%wide.region_20.23_spmd.sunk | while | flops 6328388 | bytes 246389 | solution.py:23
  1300.6 20.7 %all-gather.13 = f32[1024,129]{1,0:T(8,128)S(1)} all-gather(f32[64,129]{1,0:T(8,128)S(1)} %fusion.48), channel_id=15, replica_groups=mesh['groups'=2,'row'=16] {'row'}, dimensions={0}, use_global_device_ids=true | all-gather | bytes 561408 | tf_op jit(solution)/shard_map/all_gather | solution.py:12
  1329.5 21.1 %all-gather.14 = f32[1024,64]{1,0:T(8,128)S(1)} all-gather(f32[64,64]{1,0:T(8,128)S(1)} %copy.180), channel_id=16, replica_groups=mesh['groups'=2,'row'=16] {'row'}, dimensions={0}, use_global_device_ids=true | all-gather | bytes 278528 | tf_op jit(solution)/shard_map/all_gather | solution.py:17
  1350.6 116.1 %while.142 = (s32[]{:T(128)}, f32[64,64]{0,1:T(8,128)S(1)}, f32[16,64,64]{2,1,0:T(8,128)S(1)}, s32[]{:T(128)}, s32[]{:T(128)}, /*index=5*/s32[]{:T(128)}) while((s32[]{:T(128)}, f32[64,64]{0,1:T(8,128)S(1)}, f32[16,64,64]{2,1,0:T(8,128)S(1)}, s32[]{:T(128)}, s32[]{:T(128)}, /*index=5*/s32[]{:T(128)}) %tuple.363), condition=%wide.region_24.27_spmd, body=%wide.region_23.26_spmd.sunk | while | flops 6328388 | bytes 246389 | solution.py:23
  1472.3 18.9 %all-gather.15 = f32[1024,65]{1,0:T(8,128)S(1)} all-gather(f32[64,65]{1,0:T(8,128)S(1)} %fusion.50), channel_id=17, replica_groups=mesh['groups'=2,'row'=16] {'row'}, dimensions={0}, use_global_device_ids=true | all-gather | bytes 282880 | tf_op jit(solution)/shard_map/all_gather | solution.py:12
  1499.2 20.6 %all-gather.16 = f32[1024,64]{1,0:T(8,128)S(1)} all-gather(f32[64,64]{1,0:T(8,128)S(1)} %copy.184), channel_id=18, replica_groups=mesh['groups'=2,'row'=16] {'row'}, dimensions={0}, use_global_device_ids=true | all-gather | bytes 278528 | tf_op jit(solution)/shard_map/all_gather | solution.py:17
  1519.8 116.1 %while.143 = (s32[]{:T(128)}, f32[64,64]{0,1:T(8,128)S(1)}, f32[16,64,64]{2,1,0:T(8,128)S(1)}, s32[]{:T(128)}, s32[]{:T(128)}, /*index=5*/s32[]{:T(128)}) while((s32[]{:T(128)}, f32[64,64]{0,1:T(8,128)S(1)}, f32[16,64,64]{2,1,0:T(8,128)S(1)}, s32[]{:T(128)}, s32[]{:T(128)}, /*index=5*/s32[]{:T(128)}) %tuple.355), condition=%wide.region_27.30_spmd, body=%wide.region_26.29_spmd.sunk | while | flops 6328388 | bytes 246389 | solution.py:23
  1642.0 29.8 %all-reduce.1 = f32[1024]{0:T(1024)S(1)} all-reduce(f32[1024]{0:T(1024)S(1)} %dynamic-update-slice.2), channel_id=19, replica_groups=mesh['groups'=2,'row'=16] {'row'}, use_global_device_ids=true, to_apply=%add.1 | all-reduce | flops 1024 | bytes 8192
  (1277 shorter events, 1159.0 us)
Async XLA Ops:
  7.2 200.9 %all-gather.24.cloned.1.call-start = ((), (), s32[]{:S(2)}) async-start(), calls=%async_computation | async-start | bytes 2785280 | tf_op jit(solution)/shard_map/all_gather | solution.py:12
  167.6 233.7 %all-gather.26.cloned.1.call-start = ((), (), s32[]{:S(2)}) async-start(), calls=%async_computation.1 | async-start | bytes 2228224 | tf_op jit(solution)/shard_map/all_gather | solution.py:12
  362.5 231.6 %all-gather.28.cloned.1.call-start = ((), (), s32[]{:S(2)}) async-start(), calls=%async_computation.2 | async-start | bytes 2228224 | tf_op jit(solution)/shard_map/all_gather | solution.py:12
  555.2 229.5 %all-gather.30.cloned.1.call-start = ((), (), s32[]{:S(2)}) async-start(), calls=%async_computation.3 | async-start | bytes 1671168 | tf_op jit(solution)/shard_map/all_gather | solution.py:12
  747.7 227.3 %all-gather.32.cloned.1.call-start = ((), (), s32[]{:S(2)}) async-start(), calls=%async_computation.4 | async-start | bytes 1671168 | tf_op jit(solution)/shard_map/all_gather | solution.py:12
  815.2 123.0 %copy-start.1 = (u32[32]{0:T(128)S(1)}, u32[32]{0:T(128)}, u32[]{:S(2)}) copy-start(u32[32]{0:T(128)} %constant.375) | copy-start | bytes 388
  940.2 186.7 %copy-start = (f32[576,576]{1,0:T(8,128)}, f32[576,576]{1,0:T(8,128)S(1)}, u32[]{:S(2)}) copy-start(f32[576,576]{1,0:T(8,128)S(1)} %maximum_dynamic-update-slice_fusion.4) | copy-start | bytes 3981316
Sparse Core Ops, SparseCore 0:
  167.7 40.3 all-gather.23
  362.6 38.6 all-gather.25
  555.3 38.6 all-gather.27
  747.9 36.8 all-gather.29
  938.1 36.8 all-gather.31
